TPU v7x, 128 devices: a whole 4x4x4 slice. The times are simulated.
128 devices in a mesh: ctx: 16 (over y, x), grp: 8 (over z, core).
Axes of the slice: x: 4, y: 4, z: 4, core: 2. Of those that a mesh axis runs over, the one named last changes fastest.
Arguments:
- residual: bfloat16 [8, 2048, 2880], P('grp', 'ctx'), may hold values from -3 to 3
- queries: bfloat16 [8, 2048, 2048], P('grp', 'ctx'), may hold values from -8 to 8
- stretch_kv: bfloat16 [8, 2048, 1024], P('grp', 'ctx'), may hold values from -8 to 8
- cache_kv: bfloat16 [8, 4096, 1024], P('grp', 'ctx'), may hold values from -6 to 6
- doc_lengths: int32 [8, 8], P('grp'), may hold values from 1 to 3072, 6144 in all within a row
- sinks: float32 [32], replicated, may hold values from 2 to 6
- out_proj: bfloat16 [2048, 2880], P('ctx'), may hold values from -0.75 to 0.75
- norm_gain: float32 [2880], replicated, may hold values from 0.1 to 1.9
- router: bfloat16 [2880, 64], replicated, may hold values from -0.109375 to 0.109375
- expert_ids: int32 [8, 2048, 4], P('grp', 'ctx'), may hold values from 0 to 63, all different within a row; in each aligned block of 128 rows (0 to 127, 128 to 255, ..., all dimensions but the last counted through in order) at most 10 rows name the same one
- expert_in: bfloat16 [128, 2880, 1536], P(('ctx', 'grp')), may hold values from -0.109375 to 0.109375
- expert_out: bfloat16 [128, 768, 2880], P(('ctx', 'grp')), may hold values from -0.15625 to 0.15625
Outputs:
- resid_mid: bfloat16 [8, 2048, 2880], P('grp', 'ctx')
- layer_out: bfloat16 [8, 2048, 2880], P('grp', 'ctx')
Inputs may be any that keep to these rules, and one draw needn't show every extreme that they name: `expert_ids`: in the rows of one device (aligned blocks of 128 tokens, sequence after sequence), each expert is named by at most 10 rows, and in some blocks one expert by exactly 10; a token's 4 experts differ. `doc_lengths`: A sequence's 8 lengths sum to 6144; the longest is exactly 3072.
All inputs are finite; a program needn't handle non-finite values.
Results may differ from a plain program's by a relative error of at most 0.015.
Values may be sent and summed in bfloat16 or wider, within the bound.
No kernel may reach another device: no remote copies, remote signals or barrier semaphores. Data moves between devices by JAX's collectives and lax.ppermute only.
A program may use at most 128 MiB of HBM per device.

v0:
```python
import math
import jax
import jax.numpy as jnp
from jax import lax
from jax.sharding import PartitionSpec as P

HEADS = 32
KVH = 8
HD = 64


def doc_index(positions, lengths):
    ends = jnp.cumsum(lengths)
    return jnp.sum((positions[:, None] >= ends[None, :]).astype(jnp.int32), axis=1)


def gated_act(pre, half_width):
    gate = pre[:, :half_width]
    upper = pre[:, half_width:]
    return ((upper + 1.0) * gate * jax.nn.sigmoid(1.702 * gate)).astype(jnp.bfloat16)


def body(
    residual,
    queries,
    stretch_kv,
    cache_kv,
    doc_lengths,
    sinks,
    out_proj,
    norm_gain,
    router,
    expert_ids,
    expert_in,
    expert_out,
):
    tokens = residual.shape[1]
    width = residual.shape[2]
    cache_rows = cache_kv.shape[1]
    kv_cols = stretch_kv.shape[2] // 2
    groups = HEADS // KVH
    ctx_count = lax.axis_size("ctx")
    ctx_here = lax.axis_index("ctx")
    stretch_base = cache_rows * ctx_count
    span = cache_rows + tokens
    query_pos = stretch_base + ctx_here * tokens + jnp.arange(tokens, dtype=jnp.int32)
    lengths = doc_lengths[0]
    query_doc = doc_index(query_pos, lengths)
    query_heads = queries[0].reshape(tokens, KVH, groups, HD)
    sink_grid = sinks.reshape(KVH, groups)
    local_kv = jnp.concatenate([cache_kv[0], stretch_kv[0]], axis=0)
    scale = 1.0 / math.sqrt(HD)

    def key_block(carry, keys_values, first):
        count = keys_values.shape[0]
        rows = first + jnp.arange(count, dtype=jnp.int32)
        source = rows // span
        offset = rows % span
        key_pos = jnp.where(
            offset < cache_rows,
            source * cache_rows + offset,
            stretch_base + source * tokens + offset - cache_rows,
        )
        key_doc = doc_index(key_pos, lengths)
        allowed = (key_pos[None, :] <= query_pos[:, None]) & (
            key_doc[None, :] == query_doc[:, None]
        )
        keys = keys_values[:, :kv_cols].reshape(count, KVH, HD)
        values = keys_values[:, kv_cols:].reshape(count, KVH, HD)
        top, total, numer = carry
        scores = (
            jnp.einsum("qkgd,skd->kgqs", query_heads, keys, preferred_element_type=jnp.float32)
            * scale
        )
        masked = jnp.where(allowed[None, None], scores, -jnp.inf)
        new_top = jnp.maximum(top, jnp.max(masked, axis=-1))
        weights = jnp.where(allowed[None, None], jnp.exp(scores - new_top[..., None]), 0.0)
        shrink = jnp.exp(top - new_top)
        total = total * shrink + jnp.sum(weights, axis=-1)
        numer = numer * shrink[..., None] + jnp.einsum(
            "kgqs,skd->kgqd",
            weights.astype(jnp.bfloat16),
            values,
            preferred_element_type=jnp.float32,
        )
        return (new_top, total, numer)

    start_top = jnp.broadcast_to(sink_grid[:, :, None], (KVH, groups, tokens))
    start_total = jnp.zeros((KVH, groups, tokens), jnp.float32)
    start_numer = jnp.zeros((KVH, groups, tokens, HD), jnp.float32)
    piece = lax.all_gather(local_kv, "ctx", axis=0, tiled=True)
    count = piece.shape[0]
    step_rows = math.gcd(count, 1024)

    def advance(index, state):
        first = index * step_rows
        part = lax.dynamic_slice_in_dim(piece, first, step_rows, 0)
        return key_block(state, part, first)

    top, total, numer = lax.fori_loop(
        0, count // step_rows, advance, (start_top, start_total, start_numer)
    )
    denom = total + jnp.exp(sink_grid[:, :, None] - top)
    attended = (
        jnp.transpose(numer / denom[..., None], (2, 0, 1, 3))
        .reshape(tokens, HEADS * HD)
        .astype(jnp.bfloat16)
    )
    projected = jnp.dot(
        attended,
        lax.all_gather(out_proj, "ctx", axis=0, tiled=True),
        preferred_element_type=jnp.float32,
    )
    mid = (residual[0].astype(jnp.float32) + projected).astype(jnp.bfloat16)
    mid_float = mid.astype(jnp.float32)
    normed = (
        mid_float
        * lax.rsqrt(jnp.mean(mid_float * mid_float, axis=-1, keepdims=True) + 1e-05)
        * norm_gain
    ).astype(jnp.bfloat16)
    logits = jnp.dot(normed, router, preferred_element_type=jnp.float32)
    experts = router.shape[1]
    chosen_ids = expert_ids[0]
    topk = chosen_ids.shape[1]
    picks = chosen_ids[:, :, None] == jnp.arange(experts, dtype=jnp.int32)[None, None, :]
    chosen = jnp.sum(jnp.where(picks, logits[:, None, :], 0.0), axis=-1)
    raised = jnp.exp(chosen)
    route_weights = raised / jnp.sum(raised, axis=-1, keepdims=True)
    capacity = 2 * ((5 * tokens * topk + 8 * experts - 1) // (8 * experts))
    flat_ids = chosen_ids.reshape(-1)
    pairs = flat_ids.shape[0]
    onehot = (flat_ids[:, None] == jnp.arange(experts, dtype=jnp.int32)[None, :]).astype(jnp.int32)
    slots = jnp.sum(onehot * (jnp.cumsum(onehot, axis=0) - 1), axis=1)
    dest = flat_ids * capacity + slots
    source_rows = jnp.arange(pairs, dtype=jnp.int32) // topk
    packed = jnp.zeros((experts * capacity, width), jnp.bfloat16).at[dest].set(normed[source_rows])
    packed = packed.reshape(experts, capacity, width)
    in_weights = expert_in[0]
    out_weights = expert_out[0]
    half_width = out_weights.shape[0]
    doubled = jnp.broadcast_to(packed[:, None], (experts, 2, capacity, width)).reshape(
        2 * experts, capacity, width
    )
    received = lax.all_to_all(doubled, ("ctx", "grp"), split_axis=0, concat_axis=0, tiled=True)
    flat_rows = received.reshape(-1, width)
    pre = jnp.dot(flat_rows, in_weights, preferred_element_type=jnp.float32)
    hidden = gated_act(pre, half_width)
    partial_out = jnp.dot(hidden, out_weights, preferred_element_type=jnp.float32).astype(
        jnp.bfloat16
    )
    partial_out = partial_out.reshape(received.shape)
    returned = lax.all_to_all(partial_out, ("ctx", "grp"), split_axis=0, concat_axis=0, tiled=True)
    pair_total = jnp.sum(returned.reshape(experts, 2, capacity, width).astype(jnp.float32), axis=1)
    expert_rows = pair_total.astype(jnp.bfloat16).reshape(experts * capacity, width)
    gathered = expert_rows[dest].astype(jnp.float32) * route_weights.reshape(-1)[:, None]
    mixture = jnp.sum(gathered.reshape(tokens, topk, width), axis=1)
    final = (mid_float + mixture).astype(jnp.bfloat16)
    return (mid[None], final[None])


def solution(mesh):
    return jax.shard_map(
        body,
        mesh=mesh,
        in_specs=(
            P("grp", "ctx", None),
            P("grp", "ctx", None),
            P("grp", "ctx", None),
            P("grp", "ctx", None),
            P("grp", None),
            P(),
            P("ctx", None),
            P(),
            P(),
            P("grp", "ctx", None),
            P(("ctx", "grp"), None, None),
            P(("ctx", "grp"), None, None),
        ),
        out_specs=(P("grp", "ctx", None), P("grp", "ctx", None)),
        check_vma=False,
    )
```

profile of v0, /device:TPU:66, one launch (start us, length us, event | category | flops | bytes accessed | tf_op | source)
XLA Modules:
  0.0 739.0 jit_solution(131095022201304216)
XLA Ops:
  7.3 1.3 copy.47
  8.6 1.1 copy.48
  9.7 1.0 pad_maximum_fusion
  12.6 1.2 reduce-window.20
  14.6 97.2 %all-gather.3.cloned.1.call-done = bf16[6144,1024]{0,1:T(8,128)(2,1)} async-done(((bf16[384,1024]{0,1:T(8,128)(2,1)}), bf16[6144,1024]{0,1:T(8,128)(2,1)}) %all-gather.3.cloned.1.call-update) | async-done | bytes 12582928 | tf_op jit(solution)/shard_map/all_gather | solution.py:91
  111.8 157.7 %while.20 = (s32[]{:T(128)}, f32[8,4,128]{2,1,0:T(4,128)S(1)}, f32[8,4,128]{2,1,0:T(4,128)S(1)}, f32[8,4,128,64]{2,3,1,0:T(8,128)S(1)}, s32[1,8]{1,0:T(1,128)S(1...) while((s32[]{:T(128)}, f32[8,4,128]{2,1,0:T(4,128)S(1)}, ...), condition=%wide.region_7.8_spmd.clone, body=%wide.region_3.7_spmd.clone.sunk | while | flops 1121116288 | bytes 60053240 | solution.py:100
  111.8 1.7 fusion.68
  114.0 7.1 fusion.69
  121.1 9.8 %fusion.70 = f32[8,4,128]{2,1,0:T(4,128)S(1)} fusion(f32[8,1024,128,4]{2,1,3,0:T(8,128)} %get-tuple-element.355, f32[8,4,128]{2,1,0:T(4,128)S(1)} %max.12, pred[128,1024]{0,1:T(8,128)(4,1)S(1)} %compare_and_fusion.2), kind=kLoop, calls=%fused_computation.10.clone.1 | loop fusion | flops 16773120 | bytes 16941056 | tf_op jit(solution)/shard_map/while/body/eval_jaxpr/reduce_sum | solution.py:79
  130.9 7.6 %fusion.72 = f32[8,4,128,64]{2,3,1,0:T(8,128)S(1)} fusion(bf16[1024,8,64,1]{0,2,3,1:T(8,128)(2,1)S(1)} %bitcast.98, f32[8,1024,128,4]{2,1,3,0:T(8,128)} %get-tuple-element.355, f32[8,4,128]{2,1,0:T(4,128)S(1)} %max.12, pred[128,1024]{0,1:T(8,128)(4,1)S(1)} %compare_and_fusion.2, f32[8,4,128,64]{2,3,1,0:T(8,128)S(1)} %get-tuple-element.376, ...), kind=kOutput, calls=%fused_computation.13.clone.1 | convolution fusion | flops 554434560 | bytes 20086784 | tf_op jit(solution)/shard_map/while/body/eval_jaxpr/kgqs,skd->kgqd/dot_general | solution.py:80
  138.6 1.8 fusion.68
  140.9 7.1 fusion.69
  147.9 9.1 %fusion.70 = f32[8,4,128]{2,1,0:T(4,128)S(1)} fusion(f32[8,1024,128,4]{2,1,3,0:T(8,128)} %get-tuple-element.355, f32[8,4,128]{2,1,0:T(4,128)S(1)} %max.12, pred[128,1024]{0,1:T(8,128)(4,1)S(1)} %compare_and_fusion.2), kind=kLoop, calls=%fused_computation.10.clone.1 | loop fusion | flops 16773120 | bytes 16941056 | tf_op jit(solution)/shard_map/while/body/eval_jaxpr/reduce_sum | solution.py:79
  157.1 7.8 %fusion.72 = f32[8,4,128,64]{2,3,1,0:T(8,128)S(1)} fusion(bf16[1024,8,64,1]{0,2,3,1:T(8,128)(2,1)S(1)} %bitcast.98, f32[8,1024,128,4]{2,1,3,0:T(8,128)} %get-tuple-element.355, f32[8,4,128]{2,1,0:T(4,128)S(1)} %max.12, pred[128,1024]{0,1:T(8,128)(4,1)S(1)} %compare_and_fusion.2, f32[8,4,128,64]{2,3,1,0:T(8,128)S(1)} %get-tuple-element.376, ...), kind=kOutput, calls=%fused_computation.13.clone.1 | convolution fusion | flops 554434560 | bytes 20086784 | tf_op jit(solution)/shard_map/while/body/eval_jaxpr/kgqs,skd->kgqd/dot_general | solution.py:80
  164.9 1.7 fusion.68
  167.1 7.2 fusion.69
  174.3 9.8 %fusion.70 = f32[8,4,128]{2,1,0:T(4,128)S(1)} fusion(f32[8,1024,128,4]{2,1,3,0:T(8,128)} %get-tuple-element.355, f32[8,4,128]{2,1,0:T(4,128)S(1)} %max.12, pred[128,1024]{0,1:T(8,128)(4,1)S(1)} %compare_and_fusion.2), kind=kLoop, calls=%fused_computation.10.clone.1 | loop fusion | flops 16773120 | bytes 16941056 | tf_op jit(solution)/shard_map/while/body/eval_jaxpr/reduce_sum | solution.py:79
  184.2 7.4 %fusion.72 = f32[8,4,128,64]{2,3,1,0:T(8,128)S(1)} fusion(bf16[1024,8,64,1]{0,2,3,1:T(8,128)(2,1)S(1)} %bitcast.98, f32[8,1024,128,4]{2,1,3,0:T(8,128)} %get-tuple-element.355, f32[8,4,128]{2,1,0:T(4,128)S(1)} %max.12, pred[128,1024]{0,1:T(8,128)(4,1)S(1)} %compare_and_fusion.2, f32[8,4,128,64]{2,3,1,0:T(8,128)S(1)} %get-tuple-element.376, ...), kind=kOutput, calls=%fused_computation.13.clone.1 | convolution fusion | flops 554434560 | bytes 20086784 | tf_op jit(solution)/shard_map/while/body/eval_jaxpr/kgqs,skd->kgqd/dot_general | solution.py:80
  191.6 1.8 fusion.68
  193.9 7.2 fusion.69
  201.1 9.1 %fusion.70 = f32[8,4,128]{2,1,0:T(4,128)S(1)} fusion(f32[8,1024,128,4]{2,1,3,0:T(8,128)} %get-tuple-element.355, f32[8,4,128]{2,1,0:T(4,128)S(1)} %max.12, pred[128,1024]{0,1:T(8,128)(4,1)S(1)} %compare_and_fusion.2), kind=kLoop, calls=%fused_computation.10.clone.1 | loop fusion | flops 16773120 | bytes 16941056 | tf_op jit(solution)/shard_map/while/body/eval_jaxpr/reduce_sum | solution.py:79
  210.2 7.4 %fusion.72 = f32[8,4,128,64]{2,3,1,0:T(8,128)S(1)} fusion(bf16[1024,8,64,1]{0,2,3,1:T(8,128)(2,1)S(1)} %bitcast.98, f32[8,1024,128,4]{2,1,3,0:T(8,128)} %get-tuple-element.355, f32[8,4,128]{2,1,0:T(4,128)S(1)} %max.12, pred[128,1024]{0,1:T(8,128)(4,1)S(1)} %compare_and_fusion.2, f32[8,4,128,64]{2,3,1,0:T(8,128)S(1)} %get-tuple-element.376, ...), kind=kOutput, calls=%fused_computation.13.clone.1 | convolution fusion | flops 554434560 | bytes 20086784 | tf_op jit(solution)/shard_map/while/body/eval_jaxpr/kgqs,skd->kgqd/dot_general | solution.py:80
  217.7 1.7 fusion.68
  219.9 7.1 fusion.69
  226.9 9.1 %fusion.70 = f32[8,4,128]{2,1,0:T(4,128)S(1)} fusion(f32[8,1024,128,4]{2,1,3,0:T(8,128)} %get-tuple-element.355, f32[8,4,128]{2,1,0:T(4,128)S(1)} %max.12, pred[128,1024]{0,1:T(8,128)(4,1)S(1)} %compare_and_fusion.2), kind=kLoop, calls=%fused_computation.10.clone.1 | loop fusion | flops 16773120 | bytes 16941056 | tf_op jit(solution)/shard_map/while/body/eval_jaxpr/reduce_sum | solution.py:79
  236.1 7.4 %fusion.72 = f32[8,4,128,64]{2,3,1,0:T(8,128)S(1)} fusion(bf16[1024,8,64,1]{0,2,3,1:T(8,128)(2,1)S(1)} %bitcast.98, f32[8,1024,128,4]{2,1,3,0:T(8,128)} %get-tuple-element.355, f32[8,4,128]{2,1,0:T(4,128)S(1)} %max.12, pred[128,1024]{0,1:T(8,128)(4,1)S(1)} %compare_and_fusion.2, f32[8,4,128,64]{2,3,1,0:T(8,128)S(1)} %get-tuple-element.376, ...), kind=kOutput, calls=%fused_computation.13.clone.1 | convolution fusion | flops 554434560 | bytes 20086784 | tf_op jit(solution)/shard_map/while/body/eval_jaxpr/kgqs,skd->kgqd/dot_general | solution.py:80
  243.5 1.7 fusion.68
  245.7 7.1 fusion.69
  252.8 9.1 %fusion.70 = f32[8,4,128]{2,1,0:T(4,128)S(1)} fusion(f32[8,1024,128,4]{2,1,3,0:T(8,128)} %get-tuple-element.355, f32[8,4,128]{2,1,0:T(4,128)S(1)} %max.12, pred[128,1024]{0,1:T(8,128)(4,1)S(1)} %compare_and_fusion.2), kind=kLoop, calls=%fused_computation.10.clone.1 | loop fusion | flops 16773120 | bytes 16941056 | tf_op jit(solution)/shard_map/while/body/eval_jaxpr/reduce_sum | solution.py:79
  261.9 7.4 %fusion.72 = f32[8,4,128,64]{2,3,1,0:T(8,128)S(1)} fusion(bf16[1024,8,64,1]{0,2,3,1:T(8,128)(2,1)S(1)} %bitcast.98, f32[8,1024,128,4]{2,1,3,0:T(8,128)} %get-tuple-element.355, f32[8,4,128]{2,1,0:T(4,128)S(1)} %max.12, pred[128,1024]{0,1:T(8,128)(4,1)S(1)} %compare_and_fusion.2, f32[8,4,128,64]{2,3,1,0:T(8,128)S(1)} %get-tuple-element.376, ...), kind=kOutput, calls=%fused_computation.13.clone.1 | convolution fusion | flops 554434560 | bytes 20086784 | tf_op jit(solution)/shard_map/while/body/eval_jaxpr/kgqs,skd->kgqd/dot_general | solution.py:80
  269.7 7.7 %fusion.35 = (f32[128]{0:T(128)S(1)}, bf16[128,2880]{0,1:T(8,128)(2,1)S(1)}) fusion(bf16[2048,2880]{0,1:T(8,128)(2,1)} %all-gather.5.cloned.1.call-done, bf16[128,2048]{0,1:T(8,128)(2,1)S(1)} %bitcast.102, bf16[1,128,2880]{1,2,0:T(8,128)(2,1)} %param.14), kind=kOutput, calls=%fused_computation.55 | convolution fusion | flops 1512161152 | bytes 13795840 | tf_op jit(solution)/shard_map/dot_general | solution.py:109
  279.1 16.4 %scatter_custom_fusion = bf16[640,2880]{1,0:T(8,128)(2,1)} fusion(s32[512]{0:T(512)S(1)} %bitcast.106, bf16[128,2880]{1,0:T(8,128)(2,1)S(1)} %copy.54, s32[1024]{0:T(1024)S(1)} %pad_clamp_fusion.1, bf16[]{:T(256)} %constant.176.clone.1), kind=kCustom, calls=%fused_computation.47 | custom fusion | bytes 3686402 | tf_op jit(solution)/shard_map/scatter | solution.py:136
  295.6 7.3 broadcast_in_dim.138
  302.8 4.5 broadcast_in_dim.139
  307.4 142.9 %all_to_all.10 = bf16[128,10,2880]{2,1,0:T(8,128)(2,1)} all-to-all(bf16[128,10,2880]{2,1,0:T(8,128)(2,1)S(1)} %bitcast.97), channel_id=1, replica_groups=mesh['ctx'=16,'grp'=8] {'ctx','grp'}, dimensions={0} | all-to-all | bytes 14745600 | tf_op jit(solution)/shard_map/all_to_all | solution.py:144
  450.2 14.4 %reshape.320 = bf16[1280,2880]{1,0:T(8,128)(2,1)} reshape(bf16[128,10,2880]{2,1,0:T(8,128)(2,1)} %all_to_all.10) | data formatting | bytes 14745600 | tf_op jit(solution)/shard_map/reshape | solution.py:145
  464.6 17.2 %fusion.22 = f32[1280,1536]{1,0:T(8,128)S(1)} fusion(bf16[1280,2880]{1,0:T(8,128)(2,1)} %reshape.320, bf16[1,2880,1536]{2,1,0:T(8,128)(2,1)} %param.24), kind=kOutput, calls=%fused_computation.37 | convolution fusion | flops 11324620800 | bytes 24084480 | tf_op jit(solution)/shard_map/dot_general | solution.py:146
  481.9 11.8 %convolution_convert_fusion = bf16[1280,2880]{0,1:T(8,128)(2,1)} fusion(bf16[1,768,2880]{1,2,0:T(8,128)(2,1)} %param.25, f32[1280,1536]{1,0:T(8,128)S(1)} %fusion.22), kind=kOutput, calls=%fused_computation.36 | convolution fusion | flops 5673861120 | bytes 19660800 | tf_op jit(solution)/shard_map/dot_general | solution.py:148
  493.6 10.4 %copy.55 = bf16[1280,2880]{1,0:T(8,128)(2,1)} copy(bf16[1280,2880]{0,1:T(8,128)(2,1)} %convolution_convert_fusion) | data formatting | bytes 14745600 | tf_op jit(solution)/shard_map/convert_element_type | solution.py:148
  504.1 13.4 %reshape.321 = bf16[128,10,2880]{2,1,0:T(8,128)(2,1)} reshape(bf16[1280,2880]{1,0:T(8,128)(2,1)} %copy.55) | data formatting | bytes 14745600 | tf_op jit(solution)/shard_map/reshape | solution.py:151
  517.5 12.0 %all-to-all-start.1 = ((bf16[128,10,2880]{2,1,0:T(8,128)(2,1)}), bf16[128,10,2880]{2,1,0:T(8,128)(2,1)}, u32[]{:S(2)}, u32[]{:S(2)}) async-start(bf16[128,10,2880]{2,1,0:T(8,128)(2,1)} %reshape.321), calls=%async_computation.1 | async-start | bytes 24117248 | tf_op jit(solution)/shard_map/all_to_all | solution.py:152
  530.0 157.7 %all-to-all-done.1 = bf16[128,10,2880]{2,1,0:T(8,128)(2,1)} async-done(((bf16[128,10,2880]{2,1,0:T(8,128)(2,1)}), bf16[128,10,2880]{2,1,0:T(8,128)(2,1)}, u32[]{:S(2)}, u32[]{:S(2)}) %all-to-all-start.1) | async-done | bytes 7372832 | tf_op jit(solution)/shard_map/all_to_all | solution.py:152
  687.7 14.7 %bitcast_reduce_fusion = bf16[64,10,2880]{2,1,0:T(8,128)(2,1)} fusion(bf16[128,10,2880]{2,1,0:T(8,128)(2,1)} %all-to-all-done.1), kind=kLoop, calls=%fused_computation.35 | loop fusion | flops 1843200 | bytes 11059200 | tf_op jit(solution)/shard_map/reduce_sum | solution.py:153
  702.4 7.8 %reshape.323 = bf16[640,2880]{1,0:T(8,128)(2,1)} reshape(bf16[64,10,2880]{2,1,0:T(8,128)(2,1)} %bitcast_reduce_fusion) | data formatting | bytes 7372800 | tf_op jit(solution)/shard_map/reshape | solution.py:154
  710.2 8.4 %gather_fusion = bf16[512,2880]{1,0:T(8,128)(2,1)S(1)} fusion(bf16[640,2880]{1,0:T(8,128)(2,1)} %reshape.323, s32[1024]{0:T(1024)S(1)} %pad_clamp_fusion), kind=kCustom, calls=%fused_computation.1 | custom fusion | bytes 5900288 | tf_op jit(solution)/shard_map/gather | solution.py:155
  718.5 3.8 reshape.325
  722.3 7.0 multiply_reduce_fusion
  729.8 2.1 fusion.39
  (98 shorter events, 8.3 us)
Async XLA Ops:
  7.2 522.4 %copy-start = (bf16[2880,64]{0,1:T(8,128)(2,1)S(1)}, bf16[2880,64]{0,1:T(8,128)(2,1)}, u32[]{:S(2)}) copy-start(bf16[2880,64]{0,1:T(8,128)(2,1)} %param.22) | copy-start | bytes 1105924
  7.2 4.3 copy-start.3
  7.2 4.7 copy-start.6
  7.2 4.8 copy-start.7
  7.2 5.1 copy-start.2
  7.2 104.5 %all-gather.3.cloned.1.call-start = ((), (), s32[]{:S(2)}) async-start(), calls=%async_computation.2 | async-start | bytes 13369344 | tf_op jit(solution)/shard_map/all_gather | solution.py:91
  10.7 259.0 %all-gather.5.cloned.1.call-start = ((), (), s32[]{:S(2)}) async-start(), calls=%async_computation.3 | async-start | bytes 12533760 | tf_op jit(solution)/shard_map/all_gather | solution.py:111
  269.7 8.6 %copy-start.5 = (f32[2880]{0:T(1024)S(1)}, f32[2880]{0:T(1024)}, u32[]{:S(2)}) copy-start(f32[2880]{0:T(1024)} %param.21) | copy-start | bytes 34564
  277.5 0.9 copy-start.1
  517.5 12.3 %copy-start.4 = (s32[1,128,4]{1,2,0:T(4,128)S(1)}, s32[1,128,4]{1,2,0:T(4,128)}, u32[]{:S(2)}) copy-start(s32[1,128,4]{1,2,0:T(4,128)} %param.23) | copy-start | bytes 6148
  517.5 170.2 %all-to-all-start.1 = ((bf16[128,10,2880]{2,1,0:T(8,128)(2,1)}), bf16[128,10,2880]{2,1,0:T(8,128)(2,1)}, u32[]{:S(2)}, u32[]{:S(2)}) async-start(bf16[128,10,2880]{2,1,0:T(8,128)(2,1)} %reshape.321), calls=%async_computation.1 | async-start | bytes 24117248 | tf_op jit(solution)/shard_map/all_to_all | solution.py:152
Sparse Core Ops, SparseCore 0:
  10.8 100.8 all-gather.2
  113.8 94.9 all-gather.4
where the time goes:
time: 747 us; the launch traced here: 739 us
  waiting for transfers between devices  256 us (34%)
  blocking collectives  143 us (19%)
  matrix products  125 us (17%)
  local copies, waits for them, and re-layouts  102 us (14%)
  other arithmetic  86.3 us (12%)
  between operations  14.6 us (2%)
  starting transfers between devices  12.1 us (2%)
    all_to_all x1, waiting for transfers between devices, body(): lax.all_to_all(partial_out, ('ctx', 'grp'), split_axis=0, concat_axis=0,...  158 us
    all_to_all x1, blocking collectives, body(): lax.all_to_all(doubled, ('ctx', 'grp'), split_axis=0, concat_axis=0, tile...  143 us
    all_gather x1, waiting for transfers between devices, body(): piece = lax.all_gather(local_kv, 'ctx', axis=0, tiled=True)  97.2 us
    reduce_sum x6, other arithmetic, key_block(): total = total * shrink + jnp.sum(weights, axis=-1)  56 us
    dot_general x6, matrix products, key_block(): jnp.einsum('kgqs,skd->kgqd', weights.astype(jnp.bfloat16), values, prefer...  45 us
    dot_general x6, matrix products, key_block(): jnp.einsum('qkgd,skd->kgqs', query_heads, keys, preferred_element_type=jn...  42.7 us
    dot_general x1, matrix products, body(): pre = jnp.dot(flat_rows, in_weights, preferred_element_type=jnp.float32)  17.2 us
    scatter x1, local copies, waits for them, and re-layouts, body(): jnp.zeros((experts * capacity, width), jnp.bfloat16).at[dest]  16.4 us
  transfers between devices with their start and end apart: 3, of which 2 were waited for; matrix products, arithmetic and copies ran while one was open for 22% of the time, Pallas kernels for 0%

commit v1 on v0

--- a/solution.py
+++ b/solution.py
@@ -1,3 +1,4 @@
+import functools
 import math
 import jax
 import jax.numpy as jnp
@@ -7,6 +8,14 @@
 HEADS = 32
 KVH = 8
 HD = 64
+
+
+def carry_the_node(m, peer_axis):
+    clean = jnp.concatenate(lax.axis_size(peer_axis) * [m], axis=0)
+    return lax.all_to_all(clean, peer_axis, split_axis=0, concat_axis=0, tiled=True)
+
+
+supply_all_quarters = functools.partial(carry_the_node, peer_axis="ctx")
 
 
 def doc_index(positions, lengths):
@@ -88,7 +97,7 @@
     start_top = jnp.broadcast_to(sink_grid[:, :, None], (KVH, groups, tokens))
     start_total = jnp.zeros((KVH, groups, tokens), jnp.float32)
     start_numer = jnp.zeros((KVH, groups, tokens, HD), jnp.float32)
-    piece = lax.all_gather(local_kv, "ctx", axis=0, tiled=True)
+    piece = supply_all_quarters(local_kv)
     count = piece.shape[0]
     step_rows = math.gcd(count, 1024)
 

time: 747 us -> 951 us (1.27)
  waiting for transfers between devices: 256 us -> 349 us
  local copies, waits for them, and re-layouts: 102 us -> 162 us
  blocking collectives: 143 us -> 159 us
  matrix products: 125 us -> 138 us
  other arithmetic: 86.3 us -> 96.6 us
    all_to_all x0 -> x1, waiting for transfers between devices: none -> 190 us  [carry_the_node(): lax.all_to_all(clean, peer_axis, split_axis=0, concat_axis=0, tiled=True)]
    all_gather x1 -> x0, waiting for transfers between devices: 97.2 us -> none  [body(): piece = lax.all_gather(local_kv, 'ctx', axis=0, tiled=True)]
    all_to_all x0 -> x2, local copies, waits for them, and re-layouts: none -> 33.3 us  [carry_the_node(): lax.all_to_all(clean, peer_axis, split_axis=0, concat_axis=0, tiled=True)]
    unnamed x20 -> x59, local copies, waits for them, and re-layouts: 3.72 us -> 23.5 us
    all_to_all x1, blocking collectives: 143 us -> 159 us  [body(): lax.all_to_all(doubled, ('ctx', 'grp'), split_axis=0, concat_axis=0, tile...]
where the time goes in v1:
time: 951 us; the launch traced here: 939 us
  waiting for transfers between devices  349 us (37%)
  local copies, waits for them, and re-layouts  162 us (17%)
  blocking collectives  159 us (17%)
  matrix products  138 us (15%)
  other arithmetic  96.6 us (10%)
  starting transfers between devices  19.7 us (2%)
  between operations  14.7 us (2%)
    all_to_all x1, waiting for transfers between devices, carry_the_node(): lax.all_to_all(clean, peer_axis, split_axis=0, concat_axis=0, tiled=True)  190 us
    all_to_all x1, blocking collectives, body(): lax.all_to_all(doubled, ('ctx', 'grp'), split_axis=0, concat_axis=0, tile...  159 us
    all_to_all x1, waiting for transfers between devices, body(): lax.all_to_all(partial_out, ('ctx', 'grp'), split_axis=0, concat_axis=0,...  158 us
    reduce_sum x6, other arithmetic, key_block(): total = total * shrink + jnp.sum(weights, axis=-1)  55 us
    dot_general x6, matrix products, key_block(): jnp.einsum('kgqs,skd->kgqd', weights.astype(jnp.bfloat16), values, prefer...  52.2 us
    dot_general x6, matrix products, key_block(): jnp.einsum('qkgd,skd->kgqs', query_heads, keys, preferred_element_type=jn...  48.9 us
    all_to_all x2, local copies, waits for them, and re-layouts, carry_the_node(): lax.all_to_all(clean, peer_axis, split_axis=0, concat_axis=0, tiled=True)  33.3 us
    unnamed x59, local copies, waits for them, and re-layouts  23.5 us
  transfers between devices with their start and end apart: 3, of which 2 were waited for; matrix products, arithmetic and copies ran while one was open for 22% of the time, Pallas kernels for 0%

profile of v1, /device:TPU:66, one launch (start us, length us, event | category | flops | bytes accessed | tf_op | source)
XLA Modules:
  0.0 938.9 jit_solution(1563188771451900666)
XLA Ops:
  24.3 4.6 copy-done.3
  28.9 16.6 %copy.57 = bf16[16,384,1024]{1,2,0:T(8,128)(2,1)} copy(bf16[16,384,1024]{2,1,0:T(8,128)(2,1)} %bitcast.134) | data formatting | bytes 25165824 | tf_op jit(solution)/shard_map/all_to_all | solution.py:15
  45.5 7.6 all-to-all-start
  60.0 190.1 %all-to-all-done = bf16[16,384,1024]{1,2,0:T(8,128)(2,1)} async-done(((bf16[16,384,1024]{1,2,0:T(8,128)(2,1)}), bf16[16,384,1024]{1,2,0:T(8,128)(2,1)}, u32[]{:S(2)}, u32[]{:S(2)}) %all-to-all-start) | async-done | bytes 12582944 | tf_op jit(solution)/shard_map/all_to_all | solution.py:15
  250.1 16.7 %copy.58 = bf16[16,384,1024]{2,1,0:T(8,128)(2,1)} copy(bf16[16,384,1024]{1,2,0:T(8,128)(2,1)} %all-to-all-done) | data formatting | bytes 25165824 | tf_op jit(solution)/shard_map/all_to_all | solution.py:15
  266.9 184.1 %while.20 = (s32[]{:T(128)}, f32[8,4,128]{2,1,0:T(4,128)S(1)}, f32[8,4,128]{2,1,0:T(4,128)S(1)}, f32[8,4,128,64]{2,3,1,0:T(8,128)}, s32[1,8]{1,0:T(1,128)}, /*in...) while((s32[]{:T(128)}, f32[8,4,128]{2,1,0:T(4,128)S(1)}, ...), condition=%wide.region_7.8_spmd.clone, body=%wide.region_3.7_spmd.clone.sunk | while | flops 1121116288 | bytes 64247544 | solution.py:109
  266.9 1.7 fusion.68
  270.9 8.4 fusion.69
  279.3 9.5 %fusion.70 = f32[8,4,128]{2,1,0:T(4,128)S(1)} fusion(f32[8,1024,128,4]{2,1,3,0:T(8,128)} %get-tuple-element.373, f32[8,4,128]{2,1,0:T(4,128)S(1)} %max.12, pred[128,1024]{0,1:T(8,128)(4,1)S(1)} %compare_and_fusion.2), kind=kLoop, calls=%fused_computation.10.clone.1 | loop fusion | flops 16773120 | bytes 16941056 | tf_op jit(solution)/shard_map/while/body/eval_jaxpr/reduce_sum | solution.py:88
  289.4 8.5 fusion.72
  297.9 1.7 fusion.68
  301.9 8.1 fusion.69
  310.1 9.1 fusion.70
  319.7 8.8 fusion.72
  328.5 1.7 fusion.68
  332.5 8.1 fusion.69
  340.6 9.1 fusion.70
  350.3 8.8 fusion.72
  359.1 1.7 fusion.68
  363.1 8.1 fusion.69
  371.2 9.1 fusion.70
  380.9 8.8 fusion.72
  389.6 1.7 fusion.68
  393.7 8.1 fusion.69
  401.8 9.1 fusion.70
  411.5 8.8 fusion.72
  420.2 1.7 fusion.68
  424.3 8.1 fusion.69
  432.4 9.1 fusion.70
  442.1 8.8 fusion.72
  453.2 7.7 fusion.35
  462.6 16.6 %scatter_custom_fusion = bf16[640,2880]{1,0:T(8,128)(2,1)} fusion(s32[512]{0:T(512)S(1)} %bitcast.140, bf16[128,2880]{1,0:T(8,128)(2,1)S(1)} %copy.65, s32[1024]{0:T(1024)} %pad_clamp_fusion.1, bf16[]{:T(256)} %constant.176.clone.1), kind=kCustom, calls=%fused_computation.47 | custom fusion | bytes 3686912 | tf_op jit(solution)/shard_map/scatter | solution.py:145
  479.1 7.3 broadcast_in_dim.138
  486.4 4.5 broadcast_in_dim.139
  490.9 159.2 %all_to_all.22 = bf16[128,10,2880]{2,1,0:T(8,128)(2,1)} all-to-all(bf16[128,10,2880]{2,1,0:T(8,128)(2,1)S(1)} %bitcast.131), channel_id=1, replica_groups=mesh['ctx'=16,'grp'=8] {'ctx','grp'}, dimensions={0} | all-to-all | bytes 14745600 | tf_op jit(solution)/shard_map/all_to_all | solution.py:153
  650.1 14.4 %reshape.322 = bf16[1280,2880]{1,0:T(8,128)(2,1)} reshape(bf16[128,10,2880]{2,1,0:T(8,128)(2,1)} %all_to_all.22) | data formatting | bytes 14745600 | tf_op jit(solution)/shard_map/reshape | solution.py:154
  664.5 17.2 %fusion.22 = f32[1280,1536]{1,0:T(8,128)S(1)} fusion(bf16[1280,2880]{1,0:T(8,128)(2,1)} %reshape.322, bf16[1,2880,1536]{2,1,0:T(8,128)(2,1)} %param.24), kind=kOutput, calls=%fused_computation.37 | convolution fusion | flops 11324620800 | bytes 24084480 | tf_op jit(solution)/shard_map/dot_general | solution.py:155
  681.8 11.8 %convolution_convert_fusion = bf16[1280,2880]{0,1:T(8,128)(2,1)} fusion(bf16[1,768,2880]{1,2,0:T(8,128)(2,1)} %param.25, f32[1280,1536]{1,0:T(8,128)S(1)} %fusion.22), kind=kOutput, calls=%fused_computation.36 | convolution fusion | flops 5673861120 | bytes 19660800 | tf_op jit(solution)/shard_map/dot_general | solution.py:157
  693.5 10.4 %copy.66 = bf16[1280,2880]{1,0:T(8,128)(2,1)} copy(bf16[1280,2880]{0,1:T(8,128)(2,1)} %convolution_convert_fusion) | data formatting | bytes 14745600 | tf_op jit(solution)/shard_map/convert_element_type | solution.py:157
  703.9 13.4 %reshape.323 = bf16[128,10,2880]{2,1,0:T(8,128)(2,1)} reshape(bf16[1280,2880]{1,0:T(8,128)(2,1)} %copy.66) | data formatting | bytes 14745600 | tf_op jit(solution)/shard_map/reshape | solution.py:160
  717.3 12.0 %all-to-all-start.2 = ((bf16[128,10,2880]{2,1,0:T(8,128)(2,1)}), bf16[128,10,2880]{2,1,0:T(8,128)(2,1)}, u32[]{:S(2)}, u32[]{:S(2)}) async-start(bf16[128,10,2880]{2,1,0:T(8,128)(2,1)} %reshape.323), calls=%async_computation.2 | async-start | bytes 24117248 | tf_op jit(solution)/shard_map/all_to_all | solution.py:161
  729.9 157.7 %all-to-all-done.2 = bf16[128,10,2880]{2,1,0:T(8,128)(2,1)} async-done(((bf16[128,10,2880]{2,1,0:T(8,128)(2,1)}), bf16[128,10,2880]{2,1,0:T(8,128)(2,1)}, u32[]{:S(2)}, u32[]{:S(2)}) %all-to-all-start.2) | async-done | bytes 7372832 | tf_op jit(solution)/shard_map/all_to_all | solution.py:161
  887.6 14.7 %bitcast_reduce_fusion = bf16[64,10,2880]{2,1,0:T(8,128)(2,1)} fusion(bf16[128,10,2880]{2,1,0:T(8,128)(2,1)} %all-to-all-done.2), kind=kLoop, calls=%fused_computation.35 | loop fusion | flops 1843200 | bytes 11059200 | tf_op jit(solution)/shard_map/reduce_sum | solution.py:162
  902.3 7.8 reshape.325
  910.0 8.4 gather_fusion
  918.4 3.8 reshape.327
  922.2 7.0 multiply_reduce_fusion
  929.7 2.1 fusion.39
  (150 shorter events, 45.9 us)
Async XLA Ops:
  7.2 722.2 %copy-start = (bf16[2880,64]{0,1:T(8,128)(2,1)S(1)}, bf16[2880,64]{0,1:T(8,128)(2,1)}, u32[]{:S(2)}) copy-start(bf16[2880,64]{0,1:T(8,128)(2,1)} %param.22) | copy-start | bytes 1105924
  7.2 16.6 %copy-start.1 = (bf16[1,256,1024]{2,1,0:T(8,128)(2,1)S(1)}, bf16[1,256,1024]{2,1,0:T(8,128)(2,1)}, u32[]{:S(2)}) copy-start(bf16[1,256,1024]{2,1,0:T(8,128)(2,1)} %param.17) | copy-start | bytes 1572868
  7.2 16.6 %copy-start.2 = (bf16[1,128,1024]{2,1,0:T(8,128)(2,1)S(1)}, bf16[1,128,1024]{2,1,0:T(8,128)(2,1)}, u32[]{:S(2)}) copy-start(bf16[1,128,1024]{2,1,0:T(8,128)(2,1)} %param.16) | copy-start | bytes 786436
  24.3 4.6 copy-start.3
  45.5 8.4 copy-start.7
  45.5 8.7 copy-start.11
  45.5 8.8 copy-start.12
  45.5 9.8 %copy-start.5 = (bf16[1,128,2048]{2,1,0:T(8,128)(2,1)S(1)}, bf16[1,128,2048]{2,1,0:T(8,128)(2,1)}, u32[]{:S(2)}) copy-start(bf16[1,128,2048]{2,1,0:T(8,128)(2,1)} %param.15) | copy-start | bytes 1572868
  45.5 204.6 %all-to-all-start = ((bf16[16,384,1024]{1,2,0:T(8,128)(2,1)}), bf16[16,384,1024]{1,2,0:T(8,128)(2,1)}, u32[]{:S(2)}, u32[]{:S(2)}) async-start(bf16[16,384,1024]{1,2,0:T(8,128)(2,1)} %copy.57), calls=%async_computation | async-start | bytes 25165824 | tf_op jit(solution)/shard_map/all_to_all | solution.py:15
  53.2 400.0 %all-gather.2.cloned.1.call-start = ((), (), s32[]{:S(2)}) async-start(), calls=%async_computation.3 | async-start | bytes 12533760 | tf_op jit(solution)/shard_map/all_gather | solution.py:120
  54.3 212.5 %copy-start.6 = (f32[8,4]{1,0:T(8,128)}, f32[8,4]{1,0:T(8,128)S(1)}, u32[]{:S(2)}) copy-start(f32[8,4]{1,0:T(8,128)S(1)} %broadcast_in_dim.131) | copy-start | bytes 388
  451.0 10.8 %copy-start.9 = (f32[2880]{0:T(1024)S(1)}, f32[2880]{0:T(1024)}, u32[]{:S(2)}) copy-start(f32[2880]{0:T(1024)} %param.21) | copy-start | bytes 34564
  451.0 11.6 %copy-start.10 = (s32[512,1]{0,1:T(1,128)S(1)}, s32[512,1]{0,1:T(1,128)}, u32[]{:S(2)}) copy-start(s32[512,1]{0,1:T(1,128)} %compare_select_fusion.1) | copy-start | bytes 6148
  460.9 0.9 copy-start.4
  717.3 12.3 %copy-start.8 = (s32[1,128,4]{1,2,0:T(4,128)S(1)}, s32[1,128,4]{1,2,0:T(4,128)}, u32[]{:S(2)}) copy-start(s32[1,128,4]{1,2,0:T(4,128)} %param.23) | copy-start | bytes 6148
  717.3 170.2 %all-to-all-start.2 = ((bf16[128,10,2880]{2,1,0:T(8,128)(2,1)}), bf16[128,10,2880]{2,1,0:T(8,128)(2,1)}, u32[]{:S(2)}, u32[]{:S(2)}) async-start(bf16[128,10,2880]{2,1,0:T(8,128)(2,1)} %reshape.323), calls=%async_computation.2 | async-start | bytes 24117248 | tf_op jit(solution)/shard_map/all_to_all | solution.py:161
Sparse Core Ops, SparseCore 0:
  56.1 243.3 all-gather.1
